TPU v7x, 256 devices: a whole 4x4x8 slice. The times are simulated.
256 devices in a mesh: shard: 8 (over z), tensor: 4 (over y), section: 8 (over x, core).
Axes of the slice: x: 4, y: 4, z: 8, core: 2. Of those that a mesh axis runs over, the one named last changes fastest.
Arguments:
- emb_grad: float32 [960, 32000], P(('tensor', 'section'), 'shard'), may hold values from -60 to 60
- mlp_grad: float32 [3, 960, 2560], P(None, ('tensor', 'section'), 'shard'), may hold values from -60 to 60
- emb_basis: float32 [960, 256], P(('tensor', 'section')), may hold values from -0.1875 to 0.1875
- mlp_basis: float32 [3, 960, 256], P(None, ('tensor', 'section')), may hold values from -0.1875 to 0.1875
- emb_first: float32 [256, 32000], P(('tensor', 'section'), 'shard'), may hold values from -6 to 6
- emb_second: float32 [256, 32000], P(('tensor', 'section'), 'shard'), may hold values from 0.002 to 0.05
- mlp_first: float32 [256, 3, 2560], P(('tensor', 'section'), None, 'shard'), may hold values from -6 to 6
- mlp_second: float32 [256, 3, 2560], P(('tensor', 'section'), None, 'shard'), may hold values from 0.002 to 0.05
Outputs:
- emb_update: float32 [960, 32000], P(('tensor', 'section'), 'shard')
- mlp_update: float32 [3, 960, 2560], P(None, ('tensor', 'section'), 'shard')
- emb_first_new: float32 [256, 32000], P(('tensor', 'section'), 'shard')
- emb_second_new: float32 [256, 32000], P(('tensor', 'section'), 'shard')
- mlp_first_new: float32 [256, 3, 2560], P(('tensor', 'section'), None, 'shard')
- mlp_second_new: float32 [256, 3, 2560], P(('tensor', 'section'), None, 'shard')
- emb_basis_new: float32 [960, 256], P(('tensor', 'section'))
- mlp_basis_new: float32 [3, 960, 256], P(None, ('tensor', 'section'))
All inputs are finite; a program needn't handle non-finite values.
Results may differ from a plain program's by a relative error of at most 0.0003.
Values sent between devices are 32-bit elements; how exact they have to be, the bound alone decides.
No kernel may reach another device: no remote copies, remote signals or barrier semaphores. Data moves between devices by JAX's collectives and lax.ppermute only.
A program may use at most 64 MiB of HBM per device.

v0:
```python
import jax
import jax.numpy as jnp
from jax import lax
from jax.sharding import PartitionSpec as P

NS_STEPS = 3
coef_a = 3.4445
coef_b = -4.775
coef_c = 2.0315
bias_one = 1.0 - 0.9**10
bias_two = 1.0 - 0.999**10
adam_eps = 1e-08
norm_eps = 1e-07
highest = lax.Precision.HIGHEST


def adam_moments(first, second, projected):
    first_new = 0.9 * first + 0.1 * projected
    second_new = 0.999 * second + 0.001 * projected * projected
    direction = first_new / bias_one / (jnp.sqrt(second_new / bias_two) + adam_eps)
    return (first_new, second_new, direction)


def newton_schulz(target, gram):
    squares = jnp.trace(gram, axis1=-2, axis2=-1)
    scale = 1.0 / (jnp.sqrt(squares) + norm_eps)
    gram_term = gram * (scale * scale)[..., None, None]
    eye = jnp.eye(gram.shape[-1], dtype=gram.dtype)
    total = None
    for sweep_index in range(NS_STEPS):
        factor = coef_a * eye + polish_poly(gram_term)
        if sweep_index + 1 < NS_STEPS:
            gram_term = jnp.einsum(
                "...rs,...st->...rt",
                factor,
                jnp.einsum("...rs,...st->...rt", gram_term, factor, precision=highest),
                precision=highest,
            )
        total = (
            factor
            if total is None
            else jnp.einsum("...rs,...st->...rt", total, factor, precision=highest)
        )
    current = target * scale[..., None, None]
    return jnp.einsum("...dr,...rs->...ds", current, total, precision=highest)


def polish_poly(gram_term):
    return coef_b * gram_term + coef_c * jnp.einsum(
        "...rs,...st->...rt", gram_term, gram_term, precision=highest
    )


def gram_sums(emb_iterate, mlp_iterate):
    emb_gram = jnp.einsum("dr,ds->rs", emb_iterate, emb_iterate, precision=highest)
    mlp_gram = jnp.einsum("kdr,kds->krs", mlp_iterate, mlp_iterate, precision=highest)
    return lax.psum((emb_gram, mlp_gram), ("tensor", "section"))


def local_terms(emb_grad, mlp_grad, emb_basis, mlp_basis):
    emb_term = jnp.einsum("dr,dv->rv", emb_basis, emb_grad, precision=highest)
    mlp_term = jnp.einsum("kdr,kdf->rkf", mlp_basis, mlp_grad, precision=highest)
    return (emb_term, mlp_term)


def project_back(emb_basis, mlp_basis, emb_total, mlp_total, emb_piece, mlp_piece):
    emb_total = jnp.dot(emb_basis, emb_piece, precision=highest)
    mlp_total = jnp.einsum("kdr,rkf->kdf", mlp_basis, mlp_piece, precision=highest)
    return (emb_total, mlp_total)


def local(emb_grad, mlp_grad, emb_basis, mlp_basis, emb_first, emb_second, mlp_first, mlp_second):
    emb_term, mlp_term = local_terms(emb_grad, mlp_grad, emb_basis, mlp_basis)
    emb_zero = jnp.zeros(emb_grad.shape, jnp.float32)
    mlp_zero = jnp.zeros(mlp_grad.shape, jnp.float32)
    emb_share, mlp_share = (
        lax.psum_scatter(emb_term, ("tensor", "section"), scatter_dimension=0, tiled=True),
        lax.psum_scatter(mlp_term, ("tensor", "section"), scatter_dimension=0, tiled=True),
    )
    emb_first_new, emb_second_new, emb_direction = adam_moments(emb_first, emb_second, emb_share)
    mlp_first_new, mlp_second_new, mlp_direction = adam_moments(mlp_first, mlp_second, mlp_share)
    emb_total = emb_zero
    mlp_total = mlp_zero
    emb_piece = lax.all_gather(emb_direction, ("tensor", "section"), axis=0, tiled=True)
    emb_projected = lax.all_gather(emb_share, ("tensor", "section"), axis=0, tiled=True)
    mlp_piece = lax.all_gather(mlp_direction, ("tensor", "section"), axis=0, tiled=True)
    mlp_projected = lax.all_gather(mlp_share, ("tensor", "section"), axis=0, tiled=True)
    emb_total, mlp_total = project_back(
        emb_basis, mlp_basis, emb_total, mlp_total, emb_piece, mlp_piece
    )
    emb_found_block = jnp.einsum("dv,rv->dr", emb_grad, emb_projected, precision=highest)
    mlp_found_block = jnp.einsum("kdf,rkf->kdr", mlp_grad, mlp_projected, precision=highest)
    emb_part, mlp_part = lax.psum((emb_found_block, mlp_found_block), "shard")
    emb_gram, mlp_gram = gram_sums(emb_part, mlp_part)
    emb_iterate = newton_schulz(emb_part, emb_gram)
    mlp_iterate = newton_schulz(mlp_part, mlp_gram)
    return (
        emb_total,
        mlp_total,
        emb_first_new,
        emb_second_new,
        mlp_first_new,
        mlp_second_new,
        emb_iterate,
        mlp_iterate,
    )


def solution(mesh):
    placed = (
        P(("tensor", "section"), "shard"),
        P(None, ("tensor", "section"), "shard"),
        P(("tensor", "section"), None),
        P(None, ("tensor", "section"), None),
        P(("tensor", "section"), "shard"),
        P(("tensor", "section"), "shard"),
        P(("tensor", "section"), None, "shard"),
        P(("tensor", "section"), None, "shard"),
    )
    return jax.shard_map(
        local,
        mesh=mesh,
        in_specs=placed,
        out_specs=(
            P(("tensor", "section"), "shard"),
            P(None, ("tensor", "section"), "shard"),
            P(("tensor", "section"), "shard"),
            P(("tensor", "section"), "shard"),
            P(("tensor", "section"), None, "shard"),
            P(("tensor", "section"), None, "shard"),
            P(("tensor", "section"), None),
            P(None, ("tensor", "section"), None),
        ),
        check_vma=False,
    )
```

profile of v0, /device:TPU:1, one launch (start us, length us, event | category | flops | bytes accessed | tf_op | source)
XLA Modules:
  0.0 548.8 jit_solution(6398069834945036047)
XLA Ops:
  7.2 2.0 convolution_bitcast_fusion.1
  9.3 1.5 copy.31
  10.9 5.1 fusion.34
  17.9 113.6 %all-reduce.8.cloned.1.call-done = f32[256,3,320]{2,1,0:T(4,128)} async-done(((f32[256,3,320]{2,1,0:T(4,128)}), f32[256,3,320]{2,1,0:T(4,128)}) %all-reduce.8.cloned.1.call-update) | async-done | bytes 983056
  133.0 26.2 %all_gather.15 = f32[256,3,320]{2,0,1:T(8,128)S(1)} all-gather(f32[8,3,320]{2,0,1:T(8,128)S(1)} %get-tuple-element.31), channel_id=1, replica_groups=mesh['shard'=8,'tensor'=4,'section'=8] {'tensor','section'}, dimensions={0}, use_global_device_ids=true | all-gather | bytes 1013760 | tf_op jit(solution)/shard_map/all_gather | solution.py:87
  159.2 1.8 convolution_bitcast_fusion.3
  161.2 62.4 %reduce-scatter.2.cloned.1.call-done = f32[8,4000]{1,0:T(8,128)} async-done(((f32[256,4000]{1,0:T(8,128)}), f32[8,4000]{1,0:T(8,128)}) %reduce-scatter.2.cloned.1.call-update) | async-done | bytes 128016 | tf_op jit(solution)/shard_map/reduce_scatter | solution.py:77
  223.7 1.7 add_divide_fusion
  225.5 26.8 %all_gather.13 = f32[256,3,320]{2,0,1:T(8,128)S(1)} all-gather(f32[8,3,320]{2,0,1:T(8,128)S(1)} %get-tuple-element.28), channel_id=1, replica_groups=mesh['shard'=8,'tensor'=4,'section'=8] {'tensor','section'}, dimensions={0}, use_global_device_ids=true | all-gather | bytes 1013760 | tf_op jit(solution)/shard_map/all_gather | solution.py:86
  252.3 42.7 %all-reduce.6.cloned.1.call-done = f32[3,30,256]{2,1,0:T(8,128)} async-done(((f32[3,30,256]{2,1,0:T(8,128)}), f32[3,30,256]{2,1,0:T(8,128)}) %all-reduce.6.cloned.1.call-update) | async-done | bytes 92176 | tf_op jit(solution)/shard_map/psum | solution.py:93
  295.0 2.8 fusion.41
  297.8 54.2 %all-gather.5.cloned.1.call-done = f32[256,4000]{1,0:T(8,128)} async-done(((f32[8,4000]{1,0:T(8,128)}), f32[256,4000]{1,0:T(8,128)}) %all-gather.5.cloned.1.call-update) | async-done | bytes 4096016 | tf_op jit(solution)/shard_map/all_gather | solution.py:85
  352.0 5.9 %convolution_bitcast_fusion.4 = f32[30,256]{1,0:T(8,128)S(1)} fusion(f32[256,4000]{1,0:T(8,128)} %all-gather.5.cloned.1.call-done, f32[30,4000]{1,0:T(8,128)S(1)} %copy-done), kind=kOutput, calls=%fused_computation.22 | convolution fusion | flops 368640000 | bytes 4606720 | tf_op jit(solution)/shard_map/dv,rv->dr/dot_general | solution.py:91
  357.9 23.7 %psum.28 = f32[30,256]{1,0:T(8,128)S(1)} all-reduce(f32[30,256]{1,0:T(8,128)S(1)} %convolution_bitcast_fusion.4), channel_id=1, replica_groups=mesh['shard'=8,'tensor'=4,'section'=8] {'shard'}, use_global_device_ids=true, to_apply=%region_2.0 | all-reduce | flops 7680 | bytes 61440 | tf_op jit(solution)/shard_map/psum | solution.py:93
  381.5 1.1 fusion.35
  382.7 1.4 convolution_bitcast_fusion.2
  384.1 21.4 %all-gather.3.cloned.1.call-done = f32[256,4000]{1,0:T(8,128)} async-done(((f32[8,4000]{1,0:T(8,128)}), f32[256,4000]{1,0:T(8,128)}) %all-gather.3.cloned.1.call-update) | async-done | bytes 4096016 | tf_op jit(solution)/shard_map/all_gather | solution.py:84
  405.5 5.5 %convolution_bitcast_fusion = f32[30,4000]{1,0:T(8,128)} fusion(f32[256,4000]{1,0:T(8,128)} %all-gather.3.cloned.1.call-done, f32[30,256]{1,0:T(8,128)S(1)} %copy-done.6), kind=kOutput, calls=%fused_computation | convolution fusion | flops 368640000 | bytes 4606720 | tf_op jit(solution)/shard_map/dot_general | solution.py:67
  411.0 112.1 %all-reduce.10.cloned.1.call-done = (f32[256,256]{1,0:T(8,128)}, f32[3,256,256]{2,1,0:T(8,128)}) async-done(((f32[256,256]{1,0:T(8,128)}, f32[3,256,256]{2,1,0:T(8,128)}), (f32[256,256]{1,0:T(8,128)}, f32[3,256,256]{2,1,0:T(8,128)})) %all-reduce.10.cloned.1.call-update) | async-done | bytes 1048592 | tf_op jit(solution)/shard_map/psum | solution.py:57
  523.2 1.4 select_reduce_fusion
  524.6 2.8 fusion.5
  529.2 0.9 fusion.3
  535.7 1.1 fusion.45
  540.7 1.2 fusion.24
  (59 shorter events, 13.5 us)
Async XLA Ops:
  7.2 3.7 copy-start
  7.2 124.3 %all-reduce.8.cloned.1.call-start = ((), (), s32[]{:S(2)}) async-start(), calls=%async_computation.5 | async-start | bytes 3145728
  9.2 1.6 copy-start.6
  10.8 212.8 %reduce-scatter.2.cloned.1.call-start = ((), (), s32[]{:S(2)}) async-start(), calls=%async_computation.1 | async-start | bytes 4325376 | tf_op jit(solution)/shard_map/reduce_scatter | solution.py:77
  16.0 0.7 copy-start.11
  16.0 116.3 %copy-start.9 = (f32[8,3,320]{2,0,1:T(8,128)S(1)}, f32[8,3,320]{2,0,1:T(8,128)}, u32[]{:S(2)}) copy-start(f32[8,3,320]{2,0,1:T(8,128)} %param.14) | copy-start | bytes 92164
  16.0 116.3 %copy-start.10 = (f32[8,3,320]{2,0,1:T(8,128)S(1)}, f32[8,3,320]{2,0,1:T(8,128)}, u32[]{:S(2)}) copy-start(f32[8,3,320]{2,0,1:T(8,128)} %param.15) | copy-start | bytes 92164
  16.0 143.2 %copy-start.4 = (f32[3,30,320]{2,1,0:T(8,128)S(1)}, f32[3,30,320]{2,1,0:T(8,128)}, u32[]{:S(2)}) copy-start(f32[3,30,320]{2,1,0:T(8,128)} %param.9) | copy-start | bytes 345604
  16.0 279.0 %all-reduce.6.cloned.1.call-start = ((), (), s32[]{:S(2)}) async-start(), calls=%async_computation.4 | async-start | bytes 196608 | tf_op jit(solution)/shard_map/psum | solution.py:93
  132.3 91.4 %copy-start.7 = (f32[8,4000]{1,0:T(8,128)S(1)}, f32[8,4000]{1,0:T(8,128)}, u32[]{:S(2)}) copy-start(f32[8,4000]{1,0:T(8,128)} %param.12) | copy-start | bytes 384004
  132.3 91.4 %copy-start.8 = (f32[8,4000]{1,0:T(8,128)S(1)}, f32[8,4000]{1,0:T(8,128)}, u32[]{:S(2)}) copy-start(f32[8,4000]{1,0:T(8,128)} %param.13) | copy-start | bytes 384004
  161.1 190.9 %all-gather.5.cloned.1.call-start = ((), (), s32[]{:S(2)}) async-start(), calls=%async_computation.3 | async-start | bytes 4325376 | tf_op jit(solution)/shard_map/all_gather | solution.py:85
  223.6 181.9 %all-gather.3.cloned.1.call-start = ((), (), s32[]{:S(2)}) async-start(), calls=%async_computation.2 | async-start | bytes 4325376 | tf_op jit(solution)/shard_map/all_gather | solution.py:84
  225.4 297.8 %all-reduce.10.cloned.1.call-start = ((), (), s32[]{:S(2)}) async-start(), calls=%async_computation.6 | async-start | bytes 2097152 | tf_op jit(solution)/shard_map/psum | solution.py:57
  297.8 84.9 %copy-start.5 = (f32[3,30,256]{2,1,0:T(8,128)S(1)}, f32[3,30,256]{2,1,0:T(8,128)}, u32[]{:S(2)}) copy-start(f32[3,30,256]{2,1,0:T(8,128)} %param.11) | copy-start | bytes 276484
  523.2 4.2 copy-start.1
  531.1 1.0 copy-start.2
  538.6 2.2 copy-start.3
Sparse Core Ops, SparseCore 0:
  11.3 120.1 all-reduce.7
  135.4 88.1 reduce-scatter.1
  226.5 68.4 all-reduce.5
  297.4 54.5 all-gather.4
  355.0 50.4 all-gather.2
  408.6 114.5 all-reduce.9
where the time goes:
time: 549 us
  waiting for transfers between devices  407 us (74%)
  blocking collectives  76.7 us (14%)
  matrix products  41.5 us (8%)
  between operations  15.8 us (3%)
    unnamed x7, waiting for transfers between devices  114 us
    psum x1, waiting for transfers between devices, gram_sums(): return lax.psum((emb_gram, mlp_gram), ('tensor', 'section'))  112 us
    reduce_scatter x1, waiting for transfers between devices, local(): lax.psum_scatter(emb_term, ('tensor', 'section'), scatter_dimension=0, ti...  62.4 us
    all_gather x1, waiting for transfers between devices, local(): lax.all_gather(emb_share, ('tensor', 'section'), axis=0, tiled=True)  54.2 us
    psum x1, waiting for transfers between devices, local(): emb_part, mlp_part = lax.psum((emb_found_block, mlp_found_block), 'shard')  42.7 us
    all_gather x1, blocking collectives, local(): lax.all_gather(mlp_direction, ('tensor', 'section'), axis=0, tiled=True)  26.8 us
    all_gather x1, blocking collectives, local(): lax.all_gather(mlp_share, ('tensor', 'section'), axis=0, tiled=True)  26.2 us
    psum x1, blocking collectives, local(): emb_part, mlp_part = lax.psum((emb_found_block, mlp_found_block), 'shard')  23.7 us
  transfers between devices with their start and end apart: 6, of which 6 were waited for; matrix products, arithmetic and copies ran while one was open for 5% of the time, Pallas kernels for 0%

commit v1 on v0

--- a/solution.py
+++ b/solution.py
@@ -81,7 +81,15 @@
     mlp_first_new, mlp_second_new, mlp_direction = adam_moments(mlp_first, mlp_second, mlp_share)
     emb_total = emb_zero
     mlp_total = mlp_zero
-    emb_piece = lax.all_gather(emb_direction, ("tensor", "section"), axis=0, tiled=True)
+    emb_piece = jnp.concatenate(
+        lax.all_to_all(
+            jnp.stack([emb_direction] * lax.axis_size(("tensor", "section"))),
+            ("tensor", "section"),
+            0,
+            0,
+        ),
+        axis=0,
+    )
     emb_projected = lax.all_gather(emb_share, ("tensor", "section"), axis=0, tiled=True)
     mlp_piece = lax.all_gather(mlp_direction, ("tensor", "section"), axis=0, tiled=True)
     mlp_projected = lax.all_gather(mlp_share, ("tensor", "section"), axis=0, tiled=True)

time: 549 us -> 527 us (0.960)
  waiting for transfers between devices: 407 us -> 334 us
  blocking collectives: 76.7 us -> 118 us
  starting transfers between devices: 0.24 us -> 7.59 us
    psum x1, waiting for transfers between devices: 42.7 us -> 0.01 us  [local(): emb_part, mlp_part = lax.psum((emb_found_block, mlp_found_block), 'shard')]
    all_gather x1, blocking collectives: 26.8 us -> 68.9 us  [local(): lax.all_gather(mlp_direction, ('tensor', 'section'), axis=0, tiled=True)]
    all_gather x1 -> x0, waiting for transfers between devices: 21.4 us -> none  [local(): lax.all_gather(emb_direction, ('tensor', 'section'), axis=0, tiled=True)]
    all_gather x1, waiting for transfers between devices: 54.2 us -> 45.1 us  [local(): lax.all_gather(emb_share, ('tensor', 'section'), axis=0, tiled=True)]
    all_to_all x0 -> x1, starting transfers between devices: none -> 7.38 us  [local(): lax.all_to_all(jnp.stack([emb_direction] * lax.axis_size(('tensor', 'sect...]
    unnamed x7 -> x6, waiting for transfers between devices: 114 us -> 114 us
  transfers between devices with their start and end apart: 6 -> 6, of which waited for: 6 -> 4; matrix products, arithmetic and copies ran while one was open for 5% -> 6% of each run, Pallas kernels for 0% -> 0%
where the time goes in v1:
time: 527 us
  waiting for transfers between devices  334 us (63%)
  blocking collectives  118 us (22%)
  matrix products  41.8 us (8%)
  between operations  15.5 us (3%)
  starting transfers between devices  7.59 us (1%)
  local copies, waits for them, and re-layouts  5.42 us (1%)
    unnamed x6, waiting for transfers between devices  114 us
    psum x1, waiting for transfers between devices, gram_sums(): return lax.psum((emb_gram, mlp_gram), ('tensor', 'section'))  112 us
    all_gather x1, blocking collectives, local(): lax.all_gather(mlp_direction, ('tensor', 'section'), axis=0, tiled=True)  68.9 us
    reduce_scatter x1, waiting for transfers between devices, local(): lax.psum_scatter(emb_term, ('tensor', 'section'), scatter_dimension=0, ti...  62.5 us
    all_gather x1, waiting for transfers between devices, local(): lax.all_gather(emb_share, ('tensor', 'section'), axis=0, tiled=True)  45.1 us
    all_gather x1, blocking collectives, local(): lax.all_gather(mlp_share, ('tensor', 'section'), axis=0, tiled=True)  26.2 us
    psum x1, blocking collectives, local(): emb_part, mlp_part = lax.psum((emb_found_block, mlp_found_block), 'shard')  23.2 us
  transfers between devices with their start and end apart: 6, of which 4 were waited for; matrix products, arithmetic and copies ran while one was open for 6% of the time, Pallas kernels for 0%

profile of v1, /device:TPU:1, one launch (start us, length us, event | category | flops | bytes accessed | tf_op | source)
XLA Modules:
  0.0 526.8 jit_solution(498048346829355618)
XLA Ops:
  7.2 2.0 convolution_bitcast_fusion.1
  9.3 1.5 copy.31
  10.9 5.0 fusion.35
  17.3 114.2 %all-reduce.8.cloned.1.call-done = f32[256,3,320]{2,1,0:T(4,128)} async-done(((f32[256,3,320]{2,1,0:T(4,128)}), f32[256,3,320]{2,1,0:T(4,128)}) %all-reduce.8.cloned.1.call-update) | async-done | bytes 983056
  133.0 26.2 %all_gather.11 = f32[256,3,320]{2,0,1:T(8,128)S(1)} all-gather(f32[8,3,320]{2,0,1:T(8,128)S(1)} %get-tuple-element.31), channel_id=1, replica_groups=mesh['shard'=8,'tensor'=4,'section'=8] {'tensor','section'}, dimensions={0}, use_global_device_ids=true | all-gather | bytes 1013760 | tf_op jit(solution)/shard_map/all_gather | solution.py:95
  159.2 1.9 convolution_bitcast_fusion.3
  161.1 62.5 %reduce-scatter.2.cloned.1.call-done = f32[8,4000]{1,0:T(8,128)} async-done(((f32[256,4000]{1,0:T(8,128)}), f32[8,4000]{1,0:T(8,128)}) %reduce-scatter.2.cloned.1.call-update) | async-done | bytes 128016 | tf_op jit(solution)/shard_map/reduce_scatter | solution.py:77
  223.6 1.7 add_divide_fusion
  225.3 2.4 stack.2
  227.8 7.4 %all-to-all-start = ((f32[32,8,4000]{2,1,0:T(8,128)}), f32[32,8,4000]{2,1,0:T(8,128)}, u32[]{:S(2)}, u32[]{:S(2)}) async-start(f32[32,8,4000]{2,1,0:T(8,128)} %stack.2), calls=%async_computation.1 | async-start | bytes 8388608 | tf_op jit(solution)/shard_map/all_to_all | solution.py:85
  235.3 68.9 %all_gather.9 = f32[256,3,320]{2,0,1:T(8,128)S(1)} all-gather(f32[8,3,320]{2,0,1:T(8,128)S(1)} %get-tuple-element.28), channel_id=1, replica_groups=mesh['shard'=8,'tensor'=4,'section'=8] {'tensor','section'}, dimensions={0}, use_global_device_ids=true | all-gather | bytes 1013760 | tf_op jit(solution)/shard_map/all_gather | solution.py:94
  304.2 2.8 fusion.42
  306.9 45.1 %all-gather.2.cloned.1.call-done = f32[256,4000]{1,0:T(8,128)} async-done(((f32[8,4000]{1,0:T(8,128)}), f32[256,4000]{1,0:T(8,128)}) %all-gather.2.cloned.1.call-update) | async-done | bytes 4096016 | tf_op jit(solution)/shard_map/all_gather | solution.py:93
  352.0 5.9 %convolution_bitcast_fusion.4 = f32[30,256]{1,0:T(8,128)S(1)} fusion(f32[256,4000]{1,0:T(8,128)} %all-gather.2.cloned.1.call-done, f32[30,4000]{1,0:T(8,128)S(1)} %copy-done), kind=kOutput, calls=%fused_computation.23 | convolution fusion | flops 368640000 | bytes 4606720 | tf_op jit(solution)/shard_map/dv,rv->dr/dot_general | solution.py:99
  357.9 23.2 %psum.28 = f32[30,256]{1,0:T(8,128)S(1)} all-reduce(f32[30,256]{1,0:T(8,128)S(1)} %convolution_bitcast_fusion.4), channel_id=1, replica_groups=mesh['shard'=8,'tensor'=4,'section'=8] {'shard'}, use_global_device_ids=true, to_apply=%region_2.0 | all-reduce | flops 7680 | bytes 61440 | tf_op jit(solution)/shard_map/psum | solution.py:101
  381.0 1.1 fusion.36
  382.2 1.4 convolution_bitcast_fusion.2
  383.6 5.5 %convolution_bitcast_fusion = f32[30,4000]{1,0:T(8,128)} fusion(f32[30,256]{1,0:T(8,128)S(1)} %copy-done.5, f32[32,8,4000]{2,1,0:T(8,128)} %all-to-all-done), kind=kOutput, calls=%fused_computation | convolution fusion | flops 368640000 | bytes 4606720 | tf_op jit(solution)/shard_map/dot_general | solution.py:67
  389.2 112.1 %all-reduce.10.cloned.1.call-done = (f32[256,256]{1,0:T(8,128)}, f32[3,256,256]{2,1,0:T(8,128)}) async-done(((f32[256,256]{1,0:T(8,128)}, f32[3,256,256]{2,1,0:T(8,128)}), (f32[256,256]{1,0:T(8,128)}, f32[3,256,256]{2,1,0:T(8,128)})) %all-reduce.10.cloned.1.call-update) | async-done | bytes 1048592 | tf_op jit(solution)/shard_map/psum | solution.py:57
  501.2 1.7 select_reduce_fusion.1
  503.6 1.5 fusion.10
  505.2 1.3 fusion.20
  508.3 1.1 fusion.6
  519.1 1.2 fusion.25
  (57 shorter events, 13.7 us)
Async XLA Ops:
  7.2 3.7 copy-start
  7.2 3.7 copy-start.5
  7.2 124.3 %all-reduce.8.cloned.1.call-start = ((), (), s32[]{:S(2)}) async-start(), calls=%async_computation.5 | async-start | bytes 3145728
  10.8 5.2 copy-start.10
  10.8 121.5 %copy-start.8 = (f32[8,3,320]{2,0,1:T(8,128)S(1)}, f32[8,3,320]{2,0,1:T(8,128)}, u32[]{:S(2)}) copy-start(f32[8,3,320]{2,0,1:T(8,128)} %param.14) | copy-start | bytes 92164
  10.8 121.5 %copy-start.9 = (f32[8,3,320]{2,0,1:T(8,128)S(1)}, f32[8,3,320]{2,0,1:T(8,128)}, u32[]{:S(2)}) copy-start(f32[8,3,320]{2,0,1:T(8,128)} %param.15) | copy-start | bytes 92164
  10.8 148.4 %copy-start.3 = (f32[3,30,320]{2,1,0:T(8,128)S(1)}, f32[3,30,320]{2,1,0:T(8,128)}, u32[]{:S(2)}) copy-start(f32[3,30,320]{2,1,0:T(8,128)} %param.9) | copy-start | bytes 345604
  10.9 212.7 %reduce-scatter.2.cloned.1.call-start = ((), (), s32[]{:S(2)}) async-start(), calls=%async_computation.2 | async-start | bytes 4325376 | tf_op jit(solution)/shard_map/reduce_scatter | solution.py:77
  16.0 207.7 %copy-start.6 = (f32[8,4000]{1,0:T(8,128)S(1)}, f32[8,4000]{1,0:T(8,128)}, u32[]{:S(2)}) copy-start(f32[8,4000]{1,0:T(8,128)} %param.12) | copy-start | bytes 384004
  16.0 207.7 %copy-start.7 = (f32[8,4000]{1,0:T(8,128)S(1)}, f32[8,4000]{1,0:T(8,128)}, u32[]{:S(2)}) copy-start(f32[8,4000]{1,0:T(8,128)} %param.13) | copy-start | bytes 384004
  16.0 288.2 %all-reduce.6.cloned.1.call-start = ((), (), s32[]{:S(2)}) async-start(), calls=%async_computation.4 | async-start | bytes 196608 | tf_op jit(solution)/shard_map/psum | solution.py:101
  161.1 190.9 %all-gather.2.cloned.1.call-start = ((), (), s32[]{:S(2)}) async-start(), calls=%async_computation.3 | async-start | bytes 4325376 | tf_op jit(solution)/shard_map/all_gather | solution.py:93
  227.8 155.9 %all-to-all-start = ((f32[32,8,4000]{2,1,0:T(8,128)}), f32[32,8,4000]{2,1,0:T(8,128)}, u32[]{:S(2)}, u32[]{:S(2)}) async-start(f32[32,8,4000]{2,1,0:T(8,128)} %stack.2), calls=%async_computation.1 | async-start | bytes 8388608 | tf_op jit(solution)/shard_map/all_to_all | solution.py:85
  235.2 266.1 %all-reduce.10.cloned.1.call-start = ((), (), s32[]{:S(2)}) async-start(), calls=%async_computation.6 | async-start | bytes 2097152 | tf_op jit(solution)/shard_map/psum | solution.py:57
  235.3 146.9 %copy-start.4 = (f32[3,30,256]{2,1,0:T(8,128)S(1)}, f32[3,30,256]{2,1,0:T(8,128)}, u32[]{:S(2)}) copy-start(f32[3,30,256]{2,1,0:T(8,128)} %param.11) | copy-start | bytes 276484
  501.2 6.9 %copy-start.1 = (f32[3,256,256]{2,1,0:T(8,128)S(1)}, f32[3,256,256]{2,1,0:T(8,128)}, u32[]{:S(2)}) copy-start(f32[3,256,256]{2,1,0:T(8,128)} %get-tuple-element.25) | copy-start | bytes 2359300
  515.1 4.0 copy-start.2
Sparse Core Ops, SparseCore 0:
  11.3 120.1 all-reduce.7
  135.4 88.1 reduce-scatter.1
  226.5 68.7 all-reduce.5
  297.7 54.2 all-gather.1
  382.3 118.8 all-reduce.9
